TPU v7x, 256 devices: a whole 4x4x8 slice. The times are simulated.
256 devices in a mesh: row: 16 (over z, y_lo), col: 16 (over y_hi, x, core).
Axes of the slice: x: 4, y: 4 (y_hi: 2, y_lo: 2; y = y_hi * 2 + y_lo), z: 8, core: 2. Of those that a mesh axis runs over, the one named last changes fastest.
Arguments:
- points: float32 [32, 65536], P(None, ('row', 'col')), may hold values from -6 to 6
- candidates: float32 [32, 16384], P(None, ('row', 'col')), may hold values from -6 to 6
- length_scales: float32 [32], replicated, may hold values from 1.5 to 4
- signal_var: float32 [1], replicated, may hold values from 0.5 to 2
- noise_var: float32 [1], replicated, may hold values from 0.1 to 1
- cand_prior: float32 [16384], P(('row', 'col')), may hold values from -6 to 6
- weights: float32 [16, 65536], P(None, ('row', 'col')), may hold values from -6 to 6
- residual: float32 [16, 65536], P(None, ('row', 'col')), may hold values from -300 to 300, as said below
- direction: float32 [16, 65536], P(None, ('row', 'col')), may hold values from -300 to 300, as said below
Outputs:
- weights_new: float32 [16, 65536], P(None, ('row', 'col'))
- residual_new: float32 [16, 65536], P(None, ('row', 'col'))
- direction_new: float32 [16, 65536], P(None, ('row', 'col'))
- cand_fit: float32 [16, 16384], P(None, ('row', 'col'))
Inputs may be any that keep to these rules, and one draw needn't show every extreme that they name: `residual`: real values. `direction`: real values.
All inputs are finite; a program needn't handle non-finite values.
Results may differ from a plain program's by a relative error of at most 0.011.
Values may be sent and summed in bfloat16 or wider, within the bound.
No kernel may reach another device: no remote copies, remote signals or barrier semaphores. Data moves between devices by JAX's collectives and lax.ppermute only.
A program may use at most 64 MiB of HBM per device.

v0:
```python
import math
import jax
import jax.numpy as jnp
from jax import lax
from jax.sharding import PartitionSpec as P

root_five = math.sqrt(5.0)
contract_first = (((0,), (0,)), ((), ()))
contract_last = (((1,), (1,)), ((), ()))


def square_norms(scaled):
    return jnp.sum(jnp.square(scaled.astype(jnp.float32)), axis=0)


def matern_block(row_pts, row_sq, col_pts, col_sq, signal_scalar):
    inner_prod = lax.dot_general(
        row_pts, col_pts, contract_first, preferred_element_type=jnp.float32
    )
    dist_sq = jnp.maximum(row_sq[:, None] + col_sq[None, :] - 2.0 * inner_prod, 0.0)
    distance = jnp.sqrt(dist_sq)
    kern_vals = (
        signal_scalar
        * (1.0 + root_five * distance + 5.0 / 3.0 * dist_sq)
        * jnp.exp(-root_five * distance)
    )
    return kern_vals.astype(jnp.bfloat16)


def kernel_apply(running, row_pts, row_sq, col_pts, col_sq, vectors, signal_scalar):
    row_count = row_pts.shape[1]
    width_all = col_pts.shape[1]
    block_len = math.gcd(width_all, max(256, 1048576 // row_count))
    num_blocks = width_all // block_len

    def one_block(total, pieces):
        pts_blk, sq_blk, vec_blk = pieces
        kern_vals = matern_block(row_pts, row_sq, pts_blk, sq_blk, signal_scalar)
        return (
            total
            + lax.dot_general(
                vec_blk, kern_vals, contract_last, preferred_element_type=jnp.float32
            ),
            None,
        )

    feature_count = col_pts.shape[0]
    pts_blocks = col_pts.reshape(feature_count, num_blocks, block_len).transpose(1, 0, 2)
    sq_blocks = col_sq.reshape(num_blocks, block_len)
    vec_blocks = vectors.reshape(vectors.shape[0], num_blocks, block_len).transpose(1, 0, 2)
    result, ignored = lax.scan(one_block, running, (pts_blocks, sq_blocks, vec_blocks))
    return result


def per_device(
    points,
    candidates,
    length_scales,
    signal_var,
    noise_var,
    cand_prior,
    weights,
    residual,
    direction,
):
    scaled = (points / length_scales[:, None]).astype(jnp.bfloat16)
    cand_scaled = (candidates / length_scales[:, None]).astype(jnp.bfloat16)
    signal_scalar = signal_var[0]
    dir_low = direction.astype(jnp.bfloat16)
    col_total = direction.shape[0]
    norm_now = lax.psum(jnp.sum(residual * residual, axis=1), ("row", "col"))
    row_pts, row_cands = (
        lax.all_gather(scaled, "col", axis=1, tiled=True),
        lax.all_gather(cand_scaled, "col", axis=1, tiled=True),
    )
    col_pts = lax.all_gather(scaled, "row", axis=1, tiled=True)
    row_sq = square_norms(row_pts)
    col_sq = square_norms(col_pts)
    cand_sq = square_norms(row_cands)
    start_rows = jnp.zeros((col_total, row_pts.shape[1]), jnp.float32)
    pts_piece = col_pts
    sq_piece = col_sq
    partial_rows = kernel_apply(
        start_rows,
        row_pts,
        row_sq,
        pts_piece,
        sq_piece,
        lax.all_gather(dir_low, "row", axis=1, tiled=True),
        signal_scalar,
    )
    kernel_out = lax.psum_scatter(partial_rows, "col", scatter_dimension=1, tiled=True)
    image_vec = kernel_out + noise_var[0] * direction
    curvature = lax.psum(jnp.sum(direction * image_vec, axis=1), ("row", "col"))
    step_len = norm_now / curvature
    weights_new = weights + step_len[:, None] * direction
    residual_new = residual - step_len[:, None] * image_vec
    norm_next = lax.psum(jnp.sum(residual_new * residual_new, axis=1), ("row", "col"))
    direction_new = residual_new + (norm_next / norm_now)[:, None] * direction
    w_low = weights_new.astype(jnp.bfloat16)
    start_cands = jnp.zeros((col_total, row_cands.shape[1]), jnp.float32)
    pts_piece = col_pts
    sq_piece = col_sq
    partial_fit = kernel_apply(
        start_cands,
        row_cands,
        cand_sq,
        pts_piece,
        sq_piece,
        lax.all_gather(w_low, "row", axis=1, tiled=True),
        signal_scalar,
    )
    fitted = lax.psum_scatter(partial_fit, "col", scatter_dimension=1, tiled=True)
    cand_fit = cand_prior[None, :] + fitted
    return (weights_new, residual_new, direction_new, cand_fit)


def solution(mesh):
    placed = (
        P(None, ("row", "col")),
        P(None, ("row", "col")),
        P(),
        P(),
        P(),
        P(("row", "col")),
        P(None, ("row", "col")),
        P(None, ("row", "col")),
        P(None, ("row", "col")),
    )
    return jax.shard_map(
        per_device,
        mesh=mesh,
        in_specs=placed,
        out_specs=(
            P(None, ("row", "col")),
            P(None, ("row", "col")),
            P(None, ("row", "col")),
            P(None, ("row", "col")),
        ),
        check_vma=False,
    )
```

profile of v0, /device:TPU:2, one launch (start us, length us, event | category | flops | bytes accessed | tf_op | source)
XLA Modules:
  0.0 508.7 jit_solution(10705769252974074291)
XLA Ops:
  7.2 0.0 reduce-scatter.5.cloned.1.call-start
  7.2 0.8 divide_convert_fusion
  8.1 37.8 %all_gather.17 = bf16[32,4096]{1,0:T(8,128)(2,1)S(1)} all-gather(bf16[32,256]{1,0:T(8,128)(2,1)S(1)} %divide_convert_fusion), channel_id=1, replica_groups=mesh['row'=16,'col'=16] {'row'}, dimensions={1}, use_global_device_ids=true | all-gather | bytes 278528 | tf_op jit(solution)/shard_map/all_gather | solution.py:76
  45.9 20.4 %all_gather.16 = bf16[32,4096]{1,0:T(8,128)(2,1)S(1)} all-gather(bf16[32,256]{1,0:T(8,128)(2,1)S(1)} %divide_convert_fusion), channel_id=1, replica_groups=mesh['row'=16,'col'=16] {'col'}, dimensions={1}, use_global_device_ids=true | all-gather | bytes 278528 | tf_op jit(solution)/shard_map/all_gather | solution.py:73
  66.3 0.1 multiply_reduce_fusion
  66.4 0.1 multiply_reduce_fusion.1
  66.5 0.5 copy-done.1
  67.0 30.2 %all_gather.15 = bf16[16,4096]{1,0:T(8,128)(2,1)S(1)} all-gather(bf16[16,256]{1,0:T(8,128)(2,1)S(1)} %convert_element_type.27), channel_id=1, replica_groups=mesh['row'=16,'col'=16] {'row'}, dimensions={1}, use_global_device_ids=true | all-gather | bytes 139264 | tf_op jit(solution)/shard_map/all_gather | solution.py:89
  97.2 62.3 %while.22 = (s32[]{:T(128)}, f32[16,4096]{1,0:T(8,128)S(1)}, bf16[16,16,256]{2,1,0:T(8,128)(2,1)S(1)}, f32[]{:T(128)}, f32[4096]{0:T(1024)S(1)}, /*index=5*/f32[...) while((s32[]{:T(128)}, f32[16,4096]{1,0:T(8,128)S(1)}, ...), condition=%wide.region_5.6_spmd.clone, body=%wide.region_4.0_spmd.clone.sunk | while | flops 113377280 | bytes 832115 | solution.py:51
  97.3 3.9 convolution_add_fusion.2
  101.2 3.9 convolution_add_fusion.2
  105.1 3.8 convolution_add_fusion.2
  109.0 3.8 convolution_add_fusion.2
  112.8 3.8 convolution_add_fusion.2
  116.7 3.8 convolution_add_fusion.2
  120.6 3.8 convolution_add_fusion.2
  124.5 3.8 convolution_add_fusion.2
  128.4 3.8 convolution_add_fusion.2
  132.3 3.8 convolution_add_fusion.2
  136.2 3.8 convolution_add_fusion.2
  140.1 3.8 convolution_add_fusion.2
  144.0 3.8 convolution_add_fusion.2
  147.9 3.8 convolution_add_fusion.2
  151.8 3.8 convolution_add_fusion.2
  155.6 3.8 convolution_add_fusion.2
  159.5 0.0 copy-start
  159.5 0.0 copy-start.5
  159.5 0.0 copy-start.7
  159.5 0.7 copy-done
  160.2 0.0 reduce-scatter.5.cloned.1.call-update
  160.2 0.0 reduce-scatter.7.cloned.1.call-start
  160.3 0.0 copy-start.3
  160.3 0.2 reshape.37
  161.1 0.0 copy-done.5
  161.2 0.0 copy-done.7
  161.2 0.1 fusion.34
  161.2 24.1 %all-gather = bf16[16,64,32]{1,2,0:T(8,128)(2,1)S(1)} all-gather(bf16[1,64,32]{1,2,0:T(8,128)(2,1)S(1)} %fusion.34), channel_id=1, replica_groups=mesh['row'=16,'col'=16] {'col'}, dimensions={0}, use_global_device_ids=true | all-gather | bytes 69632 | tf_op jit(solution)/shard_map/all_gather | solution.py:74
  185.3 0.1 copy.28
  185.4 0.1 reshape.39
  185.5 0.0 copy-done.3
  185.5 0.1 multiply_reduce_fusion.5
  185.7 46.0 %reduce-scatter.5.cloned.1.call-done = f32[16,256]{1,0:T(8,128)} async-done(((f32[16,4096]{1,0:T(8,128)}), f32[16,256]{1,0:T(8,128)}) %reduce-scatter.5.cloned.1.call-update) | async-done | bytes 16400 | tf_op jit(solution)/shard_map/reduce_scatter | solution.py:92
  231.7 0.9 multiply_reduce_fusion.4
  232.6 0.1 copy.29
  232.6 73.9 %all-reduce = (f32[16]{0:T(128)S(1)}, f32[16]{0:T(128)S(1)}) all-reduce(f32[16]{0:T(128)S(1)} %multiply_reduce_fusion.5, f32[16]{0:T(128)S(1)} %multiply_reduce_fusion.4), channel_id=1, replica_groups=mesh['row'=16,'col'=16] {'row','col'}, use_global_device_ids=true, to_apply=%region_1.0 | all-reduce | flops 32 | bytes 256 | tf_op jit(solution)/shard_map/psum | solution.py:71
  306.6 0.0 copy-done.6
  306.6 0.0 copy-done.4
  306.6 0.8 multiply_reduce_fusion.3
  307.4 74.3 %psum.23 = f32[16]{0:T(128)S(1)} all-reduce(f32[16]{0:T(128)S(1)} %get-tuple-element.228), channel_id=1, replica_groups=mesh['row'=16,'col'=16] {'row','col'}, use_global_device_ids=true, to_apply=%region_10.11 | all-reduce | flops 16 | bytes 128 | tf_op jit(solution)/shard_map/psum | solution.py:98
  381.7 30.4 %all_gather.18 = bf16[16,4096]{1,0:T(8,128)(2,1)S(1)} all-gather(bf16[16,256]{1,0:T(8,128)(2,1)S(1)} %get-tuple-element.230), channel_id=1, replica_groups=mesh['row'=16,'col'=16] {'row'}, dimensions={1}, use_global_device_ids=true | all-gather | bytes 139264 | tf_op jit(solution)/shard_map/all_gather | solution.py:110
  412.1 15.4 %while.23 = (s32[]{:T(128)}, f32[16,1024]{1,0:T(8,128)S(1)}, bf16[4,16,1024]{2,1,0:T(8,128)(2,1)S(1)}, f32[]{:T(128)}, f32[1024]{0:T(1024)S(1)}, /*index=5*/f32[...) while((s32[]{:T(128)}, f32[16,1024]{1,0:T(8,128)S(1)}, ...), condition=%wide.region_13.14_spmd.clone, body=%wide.region_12.13_spmd.clone.sunk | while | flops 113278976 | bytes 312947 | solution.py:51
  412.1 3.8 fusion.51
  416.0 3.8 fusion.51
  419.8 3.8 fusion.51
  423.7 3.8 fusion.51
  427.5 0.0 copy-start.8
  427.5 1.0 copy.30
  428.5 0.0 reduce-scatter.7.cloned.1.call-update
  428.5 0.0 copy-done.2
  428.6 0.7 multiply_add_fusion
  429.2 71.2 %reduce-scatter.7.cloned.1.call-done = f32[64,16]{1,0:T(8,128)} async-done(((f32[1024,16]{1,0:T(8,128)}), f32[64,16]{1,0:T(8,128)}) %reduce-scatter.7.cloned.1.call-update) | async-done | bytes 4112
  500.4 0.8 copy.31
  501.2 0.0 copy-done.8
  501.2 0.6 broadcast_add_fusion
  (36 shorter events, 0.3 us)
Async XLA Ops:
  7.2 224.5 %reduce-scatter.5.cloned.1.call-start = ((), (), s32[]{:S(2)}) async-start(), calls=%async_computation.2 | async-start | bytes 278528 | tf_op jit(solution)/shard_map/reduce_scatter | solution.py:92
  66.3 0.7 copy-start.1
  159.5 0.7 copy-start
  159.5 1.6 copy-start.5
  159.5 1.6 copy-start.7
  160.2 340.2 %reduce-scatter.7.cloned.1.call-start = ((), (), s32[]{:S(2)}) async-start(), calls=%async_computation.3 | async-start | bytes 557056
  160.3 25.2 %copy-start.3 = (f32[16,256]{1,0:T(8,128)S(1)}, f32[16,256]{1,0:T(8,128)}, u32[]{:S(2)}) copy-start(f32[16,256]{1,0:T(8,128)} %param.20) | copy-start | bytes 49156
  185.3 121.3 %copy-start.6 = (f32[16,256]{1,0:T(8,128)S(1)}, f32[16,256]{1,0:T(8,128)}, u32[]{:S(2)}) copy-start(f32[16,256]{1,0:T(8,128)} %param.19) | copy-start | bytes 49156
  231.7 74.9 %copy-start.4 = (f32[16,256]{1,0:T(8,128)S(1)}, f32[16,256]{1,0:T(8,128)}, u32[]{:S(2)}) copy-start(f32[16,256]{1,0:T(8,128)} %reduce-scatter.5.cloned.1.call-done) | copy-start | bytes 49156
  307.4 121.2 %copy-start.2 = (f32[16,256]{1,0:T(8,128)}, f32[16,256]{1,0:T(8,128)S(1)}, u32[]{:S(2)}) copy-start(f32[16,256]{1,0:T(8,128)S(1)} %get-tuple-element.229) | copy-start | bytes 49156
  427.5 73.7 %copy-start.8 = (f32[64]{0:T(128)S(1)}, f32[64]{0:T(128)}, u32[]{:S(2)}) copy-start(f32[64]{0:T(128)} %param.18) | copy-start | bytes 772
Sparse Core Ops, SparseCore 0:
  160.3 71.2 reduce-scatter.4
  428.7 71.7 reduce-scatter.6
where the time goes:
time: 509 us
  blocking collectives  291 us (57%)
  waiting for transfers between devices  117 us (23%)
  matrix products  76.8 us (15%)
  between operations  14.9 us (3%)
    dot_general x20, matrix products, one_block(): lax.dot_general(vec_blk, kern_vals, contract_last, preferred_element_type...  76.8 us
    psum x1, blocking collectives, per_device(): lax.psum(jnp.sum(residual_new * residual_new, axis=1), ('row', 'col'))  74.3 us
    psum x1, blocking collectives, per_device(): norm_now = lax.psum(jnp.sum(residual * residual, axis=1), ('row', 'col'))  73.9 us
    unnamed x3, waiting for transfers between devices  71.2 us
    reduce_scatter x1, waiting for transfers between devices, per_device(): lax.psum_scatter(partial_rows, 'col', scatter_dimension=1, tiled=True)  46 us
    all_gather x1, blocking collectives, per_device(): col_pts = lax.all_gather(scaled, 'row', axis=1, tiled=True)  37.8 us
    all_gather x1, blocking collectives, per_device(): lax.all_gather(w_low, 'row', axis=1, tiled=True)  30.4 us
    all_gather x1, blocking collectives, per_device(): lax.all_gather(dir_low, 'row', axis=1, tiled=True)  30.2 us
  transfers between devices with their start and end apart: 2, of which 2 were waited for; matrix products, arithmetic and copies ran while one was open for 0% of the time, Pallas kernels for 0%

commit v1 on v0

--- a/solution.py
+++ b/solution.py
@@ -86,7 +86,9 @@
         row_sq,
         pts_piece,
         sq_piece,
-        lax.all_gather(dir_low, "row", axis=1, tiled=True),
+        jnp.concatenate(
+            lax.all_to_all(jnp.stack([dir_low] * lax.axis_size("row")), "row", 0, 0), axis=1
+        ),
         signal_scalar,
     )
     kernel_out = lax.psum_scatter(partial_rows, "col", scatter_dimension=1, tiled=True)

time: 509 us -> 488 us (0.959)
  blocking collectives: 291 us -> 258 us
  starting transfers between devices: 0.08 us -> 9.66 us
    all_gather x1 -> x0, blocking collectives: 30.2 us -> none  [per_device(): lax.all_gather(dir_low, 'row', axis=1, tiled=True)]
    all_to_all x0 -> x1, starting transfers between devices: none -> 9.58 us  [per_device(): lax.all_to_all(jnp.stack([dir_low] * lax.axis_size('row')), 'row', 0, 0)]
  transfers between devices with their start and end apart: 2 -> 3, of which waited for: 2 -> 2; matrix products, arithmetic and copies ran while one was open for 0% -> 0% of each run, Pallas kernels for 0% -> 0%
where the time goes in v1:
time: 488 us; the launch traced here: 487 us
  blocking collectives  258 us (53%)
  waiting for transfers between devices  118 us (24%)
  matrix products  76.8 us (16%)
  between operations  14.9 us (3%)
  starting transfers between devices  9.66 us (2%)
  other arithmetic  4.93 us (1%)
    dot_general x20, matrix products, one_block(): lax.dot_general(vec_blk, kern_vals, contract_last, preferred_element_type...  76.8 us
    psum x1, blocking collectives, per_device(): lax.psum(jnp.sum(residual_new * residual_new, axis=1), ('row', 'col'))  74.3 us
    psum x1, blocking collectives, per_device(): norm_now = lax.psum(jnp.sum(residual * residual, axis=1), ('row', 'col'))  74 us
    unnamed x3, waiting for transfers between devices  71.2 us
    reduce_scatter x1, waiting for transfers between devices, per_device(): lax.psum_scatter(partial_rows, 'col', scatter_dimension=1, tiled=True)  46.8 us
    all_gather x1, blocking collectives, per_device(): col_pts = lax.all_gather(scaled, 'row', axis=1, tiled=True)  34.9 us
    all_gather x1, blocking collectives, per_device(): lax.all_gather(w_low, 'row', axis=1, tiled=True)  30.4 us
    all_gather x1, blocking collectives, per_device(): lax.all_gather(cand_scaled, 'col', axis=1, tiled=True)  24.1 us
  transfers between devices with their start and end apart: 3, of which 2 were waited for; matrix products, arithmetic and copies ran while one was open for 0% of the time, Pallas kernels for 0%

profile of v1, /device:TPU:2, one launch (start us, length us, event | category | flops | bytes accessed | tf_op | source)
XLA Modules:
  0.0 486.8 jit_solution(6930115395424392446)
XLA Ops:
  7.2 0.7 convert_element_type.27
  7.9 0.6 stack.2
  8.5 9.6 %all-to-all-start = ((bf16[16,16,256]{2,1,0:T(8,128)(2,1)}), bf16[16,16,256]{2,1,0:T(8,128)(2,1)S(1)}, u32[]{:S(2)}, u32[]{:S(2)}) async-start(bf16[16,16,256]{2,1,0:T(8,128)(2,1)} %stack.2), calls=%async_computation | async-start | bytes 262144 | tf_op jit(solution)/shard_map/all_to_all | solution.py:90
  18.1 0.0 reduce-scatter.5.cloned.1.call-start
  18.2 0.8 divide_convert_fusion
  19.0 34.9 %all_gather.13 = bf16[32,4096]{1,0:T(8,128)(2,1)S(1)} all-gather(bf16[32,256]{1,0:T(8,128)(2,1)S(1)} %divide_convert_fusion), channel_id=1, replica_groups=mesh['row'=16,'col'=16] {'row'}, dimensions={1}, use_global_device_ids=true | all-gather | bytes 278528 | tf_op jit(solution)/shard_map/all_gather | solution.py:76
  54.0 0.1 multiply_reduce_fusion
  54.1 0.2 reshape.35
  54.9 20.5 %all_gather.12 = bf16[32,4096]{1,0:T(8,128)(2,1)S(1)} all-gather(bf16[32,256]{1,0:T(8,128)(2,1)S(1)} %divide_convert_fusion), channel_id=1, replica_groups=mesh['row'=16,'col'=16] {'col'}, dimensions={1}, use_global_device_ids=true | all-gather | bytes 278528 | tf_op jit(solution)/shard_map/all_gather | solution.py:73
  75.4 0.1 multiply_reduce_fusion.1
  75.5 0.0 all-to-all-done
  75.5 0.0 copy-start.5
  75.5 0.0 copy-start.7
  75.5 62.2 %while.22 = (s32[]{:T(128)}, f32[16,4096]{1,0:T(8,128)S(1)}, bf16[16,16,256]{2,1,0:T(8,128)(2,1)S(1)}, f32[]{:T(128)}, f32[4096]{0:T(1024)S(1)}, /*index=5*/f32[...) while((s32[]{:T(128)}, f32[16,4096]{1,0:T(8,128)S(1)}, ...), condition=%wide.region_5.6_spmd.clone, body=%wide.region_4.0_spmd.clone.sunk | while | flops 113377280 | bytes 832115 | solution.py:51
  75.6 3.8 convolution_add_fusion.2
  79.4 3.8 convolution_add_fusion.2
  83.3 3.8 convolution_add_fusion.2
  87.2 3.8 convolution_add_fusion.2
  91.1 3.8 convolution_add_fusion.2
  95.0 3.8 convolution_add_fusion.2
  98.9 3.8 convolution_add_fusion.2
  102.8 3.8 convolution_add_fusion.2
  106.6 3.8 convolution_add_fusion.2
  110.5 3.8 convolution_add_fusion.2
  114.4 3.8 convolution_add_fusion.2
  118.3 3.8 convolution_add_fusion.2
  122.2 3.8 convolution_add_fusion.2
  126.1 3.8 convolution_add_fusion.2
  130.0 3.8 convolution_add_fusion.2
  133.8 3.8 convolution_add_fusion.2
  137.7 0.0 copy-start
  137.7 0.0 copy-start.3
  137.7 0.0 copy-start.1
  137.7 0.7 copy-done
  138.4 0.0 reduce-scatter.5.cloned.1.call-update
  138.4 0.0 reduce-scatter.7.cloned.1.call-start
  138.5 0.0 copy-done.5
  138.5 0.0 copy-done.7
  138.5 0.1 fusion.34
  138.6 24.1 %all-gather = bf16[16,64,32]{1,2,0:T(8,128)(2,1)S(1)} all-gather(bf16[1,64,32]{1,2,0:T(8,128)(2,1)S(1)} %fusion.34), channel_id=1, replica_groups=mesh['row'=16,'col'=16] {'col'}, dimensions={0}, use_global_device_ids=true | all-gather | bytes 69632 | tf_op jit(solution)/shard_map/all_gather | solution.py:74
  162.6 0.1 copy.25
  162.7 0.1 reshape.37
  162.8 0.0 copy-done.3
  162.8 0.1 multiply_reduce_fusion.5
  163.0 46.8 %reduce-scatter.5.cloned.1.call-done = f32[16,256]{1,0:T(8,128)} async-done(((f32[16,4096]{1,0:T(8,128)}), f32[16,256]{1,0:T(8,128)}) %reduce-scatter.5.cloned.1.call-update) | async-done | bytes 16400 | tf_op jit(solution)/shard_map/reduce_scatter | solution.py:94
  209.8 0.9 multiply_reduce_fusion.4
  210.7 0.1 copy.26
  210.8 74.0 %all-reduce = (f32[16]{0:T(128)S(1)}, f32[16]{0:T(128)S(1)}) all-reduce(f32[16]{0:T(128)S(1)} %multiply_reduce_fusion.5, f32[16]{0:T(128)S(1)} %multiply_reduce_fusion.4), channel_id=1, replica_groups=mesh['row'=16,'col'=16] {'row','col'}, use_global_device_ids=true, to_apply=%region_1.0 | all-reduce | flops 32 | bytes 256 | tf_op jit(solution)/shard_map/psum | solution.py:71
  284.7 0.8 multiply_reduce_fusion.3
  285.5 74.3 %psum.23 = f32[16]{0:T(128)S(1)} all-reduce(f32[16]{0:T(128)S(1)} %get-tuple-element.204), channel_id=1, replica_groups=mesh['row'=16,'col'=16] {'row','col'}, use_global_device_ids=true, to_apply=%region_10.11 | all-reduce | flops 16 | bytes 128 | tf_op jit(solution)/shard_map/psum | solution.py:100
  359.9 30.4 %all_gather.14 = bf16[16,4096]{1,0:T(8,128)(2,1)S(1)} all-gather(bf16[16,256]{1,0:T(8,128)(2,1)S(1)} %get-tuple-element.206), channel_id=1, replica_groups=mesh['row'=16,'col'=16] {'row'}, dimensions={1}, use_global_device_ids=true | all-gather | bytes 139264 | tf_op jit(solution)/shard_map/all_gather | solution.py:112
  390.2 15.4 %while.23 = (s32[]{:T(128)}, f32[16,1024]{1,0:T(8,128)S(1)}, bf16[4,16,1024]{2,1,0:T(8,128)(2,1)S(1)}, f32[]{:T(128)}, f32[1024]{0:T(1024)S(1)}, /*index=5*/f32[...) while((s32[]{:T(128)}, f32[16,1024]{1,0:T(8,128)S(1)}, ...), condition=%wide.region_13.14_spmd.clone, body=%wide.region_12.13_spmd.clone.sunk | while | flops 113278976 | bytes 312947 | solution.py:51
  390.3 3.8 fusion.51
  394.1 3.8 fusion.51
  398.0 3.8 fusion.51
  401.8 3.8 fusion.51
  405.7 0.0 copy-start.8
  405.7 1.0 copy.27
  406.7 0.0 reduce-scatter.7.cloned.1.call-update
  406.7 0.0 copy-done.2
  406.7 0.7 multiply_add_fusion
  407.4 71.2 %reduce-scatter.7.cloned.1.call-done = f32[64,16]{1,0:T(8,128)} async-done(((f32[1024,16]{1,0:T(8,128)}), f32[64,16]{1,0:T(8,128)}) %reduce-scatter.7.cloned.1.call-update) | async-done | bytes 4112
  478.6 0.8 copy.28
  479.4 0.6 broadcast_add_fusion
  (36 shorter events, 0.3 us)
Async XLA Ops:
  8.5 67.0 %all-to-all-start = ((bf16[16,16,256]{2,1,0:T(8,128)(2,1)}), bf16[16,16,256]{2,1,0:T(8,128)(2,1)S(1)}, u32[]{:S(2)}, u32[]{:S(2)}) async-start(bf16[16,16,256]{2,1,0:T(8,128)(2,1)} %stack.2), calls=%async_computation | async-start | bytes 262144 | tf_op jit(solution)/shard_map/all_to_all | solution.py:90
  18.1 191.6 %reduce-scatter.5.cloned.1.call-start = ((), (), s32[]{:S(2)}) async-start(), calls=%async_computation.3 | async-start | bytes 278528 | tf_op jit(solution)/shard_map/reduce_scatter | solution.py:94
  75.5 63.0 %copy-start.5 = (f32[32,64]{1,0:T(8,128)S(1)}, f32[32,64]{1,0:T(8,128)}, u32[]{:S(2)}) copy-start(f32[32,64]{1,0:T(8,128)} %param.14) | copy-start | bytes 24580
  75.5 63.0 %copy-start.7 = (f32[32]{0:T(128)S(1)}, f32[32]{0:T(128)}, u32[]{:S(2)}) copy-start(f32[32]{0:T(128)} %param.15) | copy-start | bytes 388
  137.7 0.7 copy-start
  137.7 25.1 %copy-start.3 = (f32[16,256]{1,0:T(8,128)S(1)}, f32[16,256]{1,0:T(8,128)}, u32[]{:S(2)}) copy-start(f32[16,256]{1,0:T(8,128)} %param.20) | copy-start | bytes 49156
  137.7 72.0 %copy-start.1 = (f32[16,256]{1,0:T(8,128)S(1)}, f32[16,256]{1,0:T(8,128)}, u32[]{:S(2)}) copy-start(f32[16,256]{1,0:T(8,128)} %param.21) | copy-start | bytes 49156
  138.4 340.1 %reduce-scatter.7.cloned.1.call-start = ((), (), s32[]{:S(2)}) async-start(), calls=%async_computation.4 | async-start | bytes 557056
  162.6 122.1 %copy-start.6 = (f32[16,256]{1,0:T(8,128)S(1)}, f32[16,256]{1,0:T(8,128)}, u32[]{:S(2)}) copy-start(f32[16,256]{1,0:T(8,128)} %param.19) | copy-start | bytes 49156
  209.8 75.0 %copy-start.4 = (f32[16,256]{1,0:T(8,128)S(1)}, f32[16,256]{1,0:T(8,128)}, u32[]{:S(2)}) copy-start(f32[16,256]{1,0:T(8,128)} %reduce-scatter.5.cloned.1.call-done) | copy-start | bytes 49156
  285.5 121.2 %copy-start.2 = (f32[16,256]{1,0:T(8,128)}, f32[16,256]{1,0:T(8,128)S(1)}, u32[]{:S(2)}) copy-start(f32[16,256]{1,0:T(8,128)S(1)} %get-tuple-element.205) | copy-start | bytes 49156
  405.7 73.7 %copy-start.8 = (f32[64]{0:T(128)S(1)}, f32[64]{0:T(128)}, u32[]{:S(2)}) copy-start(f32[64]{0:T(128)} %param.18) | copy-start | bytes 772
Sparse Core Ops, SparseCore 0:
  138.5 71.1 reduce-scatter.4
  406.8 71.7 reduce-scatter.6
